TPU v7x, 32 devices: a whole 2x2x4 slice. The times are simulated.
32 devices in a mesh: ctx: 8 (over y, x, core), fsdp: 4 (over z).
Axes of the slice: x: 2, y: 2, z: 4, core: 2. Of those that a mesh axis runs over, the one named last changes fastest.
Arguments:
- hidden_in: float32 [4, 1024, 2048], P('fsdp', 'ctx'), may hold values from -6 to 6
- block_map: int32 [16], replicated, may hold values from 0 to 15, each once
- doc_ids: int32 [4, 1024], P('fsdp'), may hold values from 0 to 3, never falling along the last dimension, each value on 1 to 512 neighbouring positions
- routes: int32 [4, 1024, 8], P('fsdp', 'ctx'), may hold values from 0 to 15, all different within a row; in each aligned block of 128 rows (0 to 127, 128 to 255, ..., all dimensions but the last counted through in order) at most 96 rows name the same one
- attn_gain: float32 [2048], replicated, may hold values from 0.5 to 1.5
- query_proj: bfloat16 [2048, 4096], P('fsdp'), may hold values from -0.125 to 0.125
- key_proj: bfloat16 [2048, 512], P('fsdp'), may hold values from -0.125 to 0.125
- value_proj: bfloat16 [2048, 512], P('fsdp'), may hold values from -0.125 to 0.125
- query_gain: float32 [128], replicated, may hold values from 0.1 to 1.9
- key_gain: float32 [128], replicated, may hold values from 0.1 to 1.9
- out_proj: bfloat16 [4096, 2048], P('fsdp'), may hold values from -0.375 to 0.375
- ffn_gain: float32 [2048], replicated, may hold values from 0.5 to 1.5
- router_proj: bfloat16 [2048, 16], P('fsdp'), may hold values from -0.125 to 0.125
- expert_gate: bfloat16 [16, 2048, 768], P('ctx', 'fsdp'), may hold values from -0.125 to 0.125
- expert_up: bfloat16 [16, 2048, 768], P('ctx', 'fsdp'), may hold values from -0.125 to 0.125
- expert_down: bfloat16 [16, 768, 2048], P('ctx', 'fsdp'), may hold values from -0.4375 to 0.4375
- cotangent: float32 [4, 1024, 2048], P('fsdp', 'ctx'), may hold values from -6 to 6
Outputs:
- layer_out: float32 [4, 1024, 2048], P('fsdp', 'ctx')
- input_grad: float32 [4, 1024, 2048], P('fsdp', 'ctx')
- attn_gain_grad: float32 [2048], replicated
- query_proj_grad: float32 [2048, 4096], P('fsdp')
- key_proj_grad: float32 [2048, 512], P('fsdp')
- value_proj_grad: float32 [2048, 512], P('fsdp')
- query_gain_grad: float32 [128], replicated
- key_gain_grad: float32 [128], replicated
- out_proj_grad: float32 [4096, 2048], P('fsdp')
- ffn_gain_grad: float32 [2048], replicated
- router_grad: float32 [2048, 16], P('fsdp')
- gate_grad: float32 [16, 2048, 768], P('ctx', 'fsdp')
- up_grad: float32 [16, 2048, 768], P('ctx', 'fsdp')
- down_grad: float32 [16, 768, 2048], P('ctx', 'fsdp')
Inputs may be any that keep to these rules, and one draw needn't show every extreme that they name: `block_map`: A permutation: every block of positions is held by exactly one stored block. `doc_ids`: along the positions of a sequence the document numbers never fall; each document is 1 to 512 positions long and one is exactly that long. `routes`: each token names 8 different experts. Within the 128 stored rows of one device (aligned blocks of rows), no expert is named by more than 96 of them, and in every draw some expert is named by exactly 96.
All inputs are finite; a program needn't handle non-finite values.
Results may differ from a plain program's by a relative error of at most 0.024.
Values may be sent and summed in bfloat16 or wider, within the bound.
No kernel may reach another device: no remote copies, remote signals or barrier semaphores. Data moves between devices by JAX's collectives and lax.ppermute only.
A program may use at most 320 MiB of HBM per device.

v0:
```python
import jax
import jax.numpy as jnp
from jax import lax
from jax.sharding import PartitionSpec as P

D = 2048
HEADS = 32
KV_HEADS = 4
HEAD_DIM = 128
TOP = 8
EPSILON = 1e-06
ROPE_BASE = 1000000.0
NEG_FILL = -1e30


def matmul(left, right):
    return jnp.dot(left, right, preferred_element_type=jnp.float32)


def contract(form, left, right):
    return jnp.einsum(form, left, right, preferred_element_type=jnp.float32)


def rms_scale(field):
    return lax.rsqrt(jnp.mean(field * field, axis=-1, keepdims=True) + EPSILON)


def rotary(positions):
    halfway = HEAD_DIM // 2
    inverse = ROPE_BASE ** (-2.0 * jnp.arange(halfway, dtype=jnp.float32) / HEAD_DIM)
    angle = positions.astype(jnp.float32)[:, None] * inverse[None, :]
    return (jnp.cos(angle), jnp.sin(angle))


def rotate(field, cosine, sine_table):
    halfway = field.shape[-1] // 2
    former = field[..., :halfway]
    latter = field[..., halfway:]
    cos_b = cosine[:, None, :]
    sin_b = sine_table[:, None, :]
    return jnp.concatenate(
        [former * cos_b - latter * sin_b, latter * cos_b + former * sin_b], axis=-1
    )


def rotate_back(field, cosine, sine_table):
    halfway = field.shape[-1] // 2
    former = field[..., :halfway]
    latter = field[..., halfway:]
    cos_b = cosine[:, None, :]
    sin_b = sine_table[:, None, :]
    return jnp.concatenate(
        [former * cos_b + latter * sin_b, latter * cos_b - former * sin_b], axis=-1
    )


def norm_back(grad, normed, inv_scale, factor):
    lead_axes = tuple(range(grad.ndim - 1))
    factor_grad = jnp.sum(grad * normed, axis=lead_axes)
    scaled = grad * factor
    return (
        inv_scale * (scaled - normed * jnp.mean(scaled * normed, axis=-1, keepdims=True)),
        factor_grad,
    )


def per_device(
    hidden_in,
    block_map,
    doc_ids,
    routes,
    attn_gain,
    query_proj,
    key_proj,
    value_proj,
    query_gain,
    key_gain,
    out_proj,
    ffn_gain,
    router_proj,
    expert_gate,
    expert_up,
    expert_down,
    cotangent,
):
    tokens = hidden_in.shape[1]
    ctx_size = lax.axis_size("ctx")
    local_experts = expert_gate.shape[0]
    experts = local_experts * ctx_size
    capacity = min(tokens, 3 * tokens * TOP // (2 * experts))
    block_len = tokens // 2
    group_size = HEADS // KV_HEADS
    score_scale = HEAD_DIM ** (-0.5)
    ctx_index = lax.axis_index("ctx")
    own_blocks = lax.dynamic_slice_in_dim(block_map, 2 * ctx_index, 2, 0)
    offsets = jnp.arange(block_len, dtype=jnp.int32)
    local_pos = (own_blocks[:, None] * block_len + offsets[None, :]).reshape(-1)
    all_pos = (block_map[:, None] * block_len + offsets[None, :]).reshape(-1)
    doc_row = doc_ids[0]
    same_doc = jnp.take(doc_row, all_pos)[None, :] == jnp.take(doc_row, local_pos)[:, None]
    visible = (all_pos[None, :] <= local_pos[:, None]) & same_doc
    cosine, sine_table = rotary(local_pos)
    hidden = hidden_in[0]
    first_scale = rms_scale(hidden)
    first_normed = hidden * first_scale
    first_input = (first_normed * attn_gain).astype(jnp.bfloat16)
    w_query, w_key, w_value, w_out = (
        lax.all_gather(query_proj, "fsdp", axis=0, tiled=True),
        lax.all_gather(key_proj, "fsdp", axis=0, tiled=True),
        lax.all_gather(value_proj, "fsdp", axis=0, tiled=True),
        lax.all_gather(out_proj, "fsdp", axis=0, tiled=True),
    )
    query_raw = matmul(first_input, w_query).reshape(tokens, HEADS, HEAD_DIM)
    key_raw = matmul(first_input, w_key).reshape(tokens, KV_HEADS, HEAD_DIM)
    value_low = matmul(first_input, w_value).astype(jnp.bfloat16)
    query_scale = rms_scale(query_raw)
    query_normed = query_raw * query_scale
    query_rot = rotate(query_normed * query_gain, cosine, sine_table).astype(jnp.bfloat16)
    key_scale = rms_scale(key_raw)
    key_normed = key_raw * key_scale
    key_rot = (
        rotate(key_normed * key_gain, cosine, sine_table)
        .reshape(tokens, KV_HEADS * HEAD_DIM)
        .astype(jnp.bfloat16)
    )
    keys_all, values_all = (
        lax.all_gather(key_rot, "ctx", axis=0, tiled=True),
        lax.all_gather(value_low, "ctx", axis=0, tiled=True),
    )

    def split_keys(flat):
        return flat.reshape(-1, KV_HEADS, HEAD_DIM).transpose(1, 0, 2)

    def join_keys(stacked):
        return stacked.transpose(1, 0, 2).reshape(-1, KV_HEADS * HEAD_DIM)

    def split_queries(flat):
        return flat.reshape(tokens, KV_HEADS, group_size, HEAD_DIM).transpose(1, 2, 0, 3)

    def join_queries(stacked):
        return stacked.transpose(2, 0, 1, 3).reshape(tokens, HEADS * HEAD_DIM)

    def masked_scores(q_block, k_block):
        scores = contract("gtd,sd->gts", q_block, k_block) * score_scale
        return jnp.where(visible[None], scores, NEG_FILL)

    def head_forward(items):
        q_block, k_block, v_block = items
        scores = masked_scores(q_block, k_block)
        peak = jnp.max(scores, axis=-1, keepdims=True)
        expo = jnp.exp(scores - peak)
        total = jnp.sum(expo, axis=-1, keepdims=True)
        probs = (expo / total).astype(jnp.bfloat16)
        mixed = contract("gts,sd->gtd", probs, v_block)
        return (mixed, (peak + jnp.log(total))[..., 0])

    query_groups = split_queries(query_rot)
    attn_out, log_sums = lax.map(
        head_forward, (query_groups, split_keys(keys_all), split_keys(values_all))
    )
    attended = join_queries(attn_out).astype(jnp.bfloat16)
    middle = hidden + matmul(attended, w_out)
    second_scale = rms_scale(middle)
    second_normed = middle * second_scale
    second_input = (second_normed * ffn_gain).astype(jnp.bfloat16)
    w_gate, w_up, w_down, w_router = (
        lax.all_gather(expert_gate, "fsdp", axis=1, tiled=True),
        lax.all_gather(expert_up, "fsdp", axis=1, tiled=True),
        lax.all_gather(expert_down, "fsdp", axis=1, tiled=True),
        lax.all_gather(router_proj, "fsdp", axis=0, tiled=True),
    )
    logits = matmul(second_input, w_router)
    route_ids = routes[0]
    chosen = jnp.take_along_axis(logits, route_ids, axis=1)
    route_weights = jax.nn.softmax(chosen, axis=-1)
    flat_ids = route_ids.reshape(-1)
    expert_range = jnp.arange(experts, dtype=jnp.int32)
    one_hot = (flat_ids[:, None] == expert_range[None, :]).astype(jnp.int32)
    earlier = jnp.cumsum(one_hot, axis=0) - one_hot
    slot_index = jnp.sum(earlier * one_hot, axis=1)
    target = flat_ids * capacity + slot_index

    def dispatch(route_rows):
        buffer = jnp.zeros((experts * capacity, D), jnp.bfloat16).at[target].set(route_rows)
        return buffer.reshape(ctx_size, local_experts, capacity, D)

    def collect(returned):
        return jnp.take(returned.reshape(experts * capacity, D), target, axis=0)

    received = lax.all_to_all(
        dispatch(jnp.repeat(second_input, TOP, axis=0)),
        "ctx",
        split_axis=0,
        concat_axis=2,
        tiled=True,
    )[0]
    gate_val = contract("erd,edf->erf", received, w_gate)
    up_val = contract("erd,edf->erf", received, w_up)
    gate_sig = jax.nn.sigmoid(gate_val)
    hid_low = (gate_val * gate_sig * up_val).astype(jnp.bfloat16)
    expert_out = contract("erf,efd->erd", hid_low, w_down).astype(jnp.bfloat16)
    route_out = (
        collect(lax.all_to_all(expert_out[None], "ctx", split_axis=2, concat_axis=0, tiled=True))
        .reshape(tokens, TOP, D)
        .astype(jnp.float32)
    )
    layer_out = middle + jnp.einsum("tr,trd->td", route_weights, route_out)
    grad_out = cotangent[0]
    grad_weights = jnp.einsum("td,trd->tr", grad_out, route_out)
    grad_routes = (
        (route_weights[:, :, None] * grad_out[:, None, :])
        .astype(jnp.bfloat16)
        .reshape(tokens * TOP, D)
    )
    grad_expert = lax.all_to_all(
        dispatch(grad_routes), "ctx", split_axis=0, concat_axis=2, tiled=True
    )[0]
    grad_hid = contract("erd,efd->erf", grad_expert, w_down)
    down_grad_full = contract("erf,erd->efd", hid_low, grad_expert)
    grad_gate = (grad_hid * up_val * gate_sig * (1.0 + gate_val * (1.0 - gate_sig))).astype(
        jnp.bfloat16
    )
    grad_up = (grad_hid * gate_val * gate_sig).astype(jnp.bfloat16)
    gate_grad_full = contract("erd,erf->edf", received, grad_gate)
    up_grad_full = contract("erd,erf->edf", received, grad_up)
    grad_rows = (
        contract("erf,edf->erd", grad_gate, w_gate) + contract("erf,edf->erd", grad_up, w_up)
    ).astype(jnp.bfloat16)
    grad_copies = collect(
        lax.all_to_all(grad_rows[None], "ctx", split_axis=2, concat_axis=0, tiled=True)
    ).reshape(tokens, TOP, D)
    grad_chosen = route_weights * (
        grad_weights - jnp.sum(route_weights * grad_weights, axis=-1, keepdims=True)
    )
    route_hot = (route_ids[:, :, None] == expert_range[None, None, :]).astype(jnp.float32)
    grad_logits = jnp.einsum("tr,tre->te", grad_chosen, route_hot).astype(jnp.bfloat16)
    router_grad_full = contract("td,te->de", second_input, grad_logits)
    grad_second = jnp.sum(grad_copies.astype(jnp.float32), axis=1) + contract(
        "te,de->td", grad_logits, w_router
    )
    grad_middle, ffn_gain_grad = norm_back(grad_second, second_normed, second_scale, ffn_gain)
    grad_middle = grad_middle + grad_out
    w_query, w_key, w_value, w_out = (
        lax.all_gather(query_proj, "fsdp", axis=0, tiled=True),
        lax.all_gather(key_proj, "fsdp", axis=0, tiled=True),
        lax.all_gather(value_proj, "fsdp", axis=0, tiled=True),
        lax.all_gather(out_proj, "fsdp", axis=0, tiled=True),
    )
    keys_all, values_all = (
        lax.all_gather(key_rot, "ctx", axis=0, tiled=True),
        lax.all_gather(value_low, "ctx", axis=0, tiled=True),
    )
    grad_branch = grad_middle.astype(jnp.bfloat16)
    out_grad_full = contract("tq,td->qd", attended, grad_branch)
    grad_attended = contract("td,qd->tq", grad_branch, w_out).astype(jnp.bfloat16)

    def head_backward(items):
        q_block, k_block, v_block, g_block, lse_block = items
        probs = jnp.exp(masked_scores(q_block, k_block) - lse_block[..., None])
        grad_probs = contract("gtd,sd->gts", g_block, v_block)
        delta = jnp.sum(probs * grad_probs, axis=-1, keepdims=True)
        grad_scores = (probs * (grad_probs - delta)).astype(jnp.bfloat16)
        grad_q = contract("gts,sd->gtd", grad_scores, k_block) * score_scale
        grad_k = contract("gts,gtd->sd", grad_scores, q_block) * score_scale
        grad_v = contract("gts,gtd->sd", probs.astype(jnp.bfloat16), g_block)
        return (grad_q, grad_k, grad_v)

    grad_qgroups, grad_kheads, grad_vheads = lax.map(
        head_backward,
        (
            query_groups,
            split_keys(keys_all),
            split_keys(values_all),
            split_queries(grad_attended),
            log_sums,
        ),
    )
    grad_key_rot, grad_value = (
        lax.psum_scatter(
            join_keys(grad_kheads).astype(jnp.bfloat16), "ctx", scatter_dimension=0, tiled=True
        ).astype(jnp.float32),
        lax.psum_scatter(
            join_keys(grad_vheads).astype(jnp.bfloat16), "ctx", scatter_dimension=0, tiled=True
        ).astype(jnp.float32),
    )
    grad_query_rot = join_queries(grad_qgroups).reshape(tokens, HEADS, HEAD_DIM)
    grad_query, query_gain_grad = norm_back(
        rotate_back(grad_query_rot, cosine, sine_table), query_normed, query_scale, query_gain
    )
    grad_key, key_gain_grad = norm_back(
        rotate_back(grad_key_rot.reshape(tokens, KV_HEADS, HEAD_DIM), cosine, sine_table),
        key_normed,
        key_scale,
        key_gain,
    )
    grad_query = grad_query.reshape(tokens, HEADS * HEAD_DIM).astype(jnp.bfloat16)
    grad_key = grad_key.reshape(tokens, KV_HEADS * HEAD_DIM).astype(jnp.bfloat16)
    grad_value = grad_value.astype(jnp.bfloat16)
    query_grad_full = contract("td,tq->dq", first_input, grad_query)
    key_grad_full = contract("td,tq->dq", first_input, grad_key)
    value_grad_full = contract("td,tq->dq", first_input, grad_value)
    grad_first = (
        contract("tq,dq->td", grad_query, w_query)
        + contract("tq,dq->td", grad_key, w_key)
        + contract("tq,dq->td", grad_value, w_value)
    )
    grad_hidden, attn_gain_grad = norm_back(grad_first, first_normed, first_scale, attn_gain)
    grad_hidden = grad_hidden + grad_middle
    gate_grad, up_grad, down_grad = (
        lax.psum_scatter(
            gate_grad_full.astype(jnp.bfloat16), "fsdp", scatter_dimension=1, tiled=True
        ).astype(jnp.float32),
        lax.psum_scatter(
            up_grad_full.astype(jnp.bfloat16), "fsdp", scatter_dimension=1, tiled=True
        ).astype(jnp.float32),
        lax.psum_scatter(
            down_grad_full.astype(jnp.bfloat16), "fsdp", scatter_dimension=1, tiled=True
        ).astype(jnp.float32),
    )
    shard_grads = (
        lax.psum_scatter(
            query_grad_full.astype(jnp.bfloat16), "fsdp", scatter_dimension=0, tiled=True
        ).astype(jnp.float32),
        lax.psum_scatter(
            key_grad_full.astype(jnp.bfloat16), "fsdp", scatter_dimension=0, tiled=True
        ).astype(jnp.float32),
        lax.psum_scatter(
            value_grad_full.astype(jnp.bfloat16), "fsdp", scatter_dimension=0, tiled=True
        ).astype(jnp.float32),
        lax.psum_scatter(
            out_grad_full.astype(jnp.bfloat16), "fsdp", scatter_dimension=0, tiled=True
        ).astype(jnp.float32),
        lax.psum_scatter(
            router_grad_full.astype(jnp.bfloat16), "fsdp", scatter_dimension=0, tiled=True
        ).astype(jnp.float32),
    )
    query_grad, key_grad, value_grad, out_grad, router_grad = (
        lax.psum(shard_grads[0].astype(jnp.bfloat16), "ctx").astype(jnp.float32),
        lax.psum(shard_grads[1].astype(jnp.bfloat16), "ctx").astype(jnp.float32),
        lax.psum(shard_grads[2].astype(jnp.bfloat16), "ctx").astype(jnp.float32),
        lax.psum(shard_grads[3].astype(jnp.bfloat16), "ctx").astype(jnp.float32),
        lax.psum(shard_grads[4].astype(jnp.bfloat16), "ctx").astype(jnp.float32),
    )
    attn_gain_total, query_gain_total, key_gain_total, ffn_gain_total = lax.psum(
        (attn_gain_grad, query_gain_grad, key_gain_grad, ffn_gain_grad), ("ctx", "fsdp")
    )
    return (
        layer_out[None],
        grad_hidden[None],
        attn_gain_total,
        query_grad,
        key_grad,
        value_grad,
        query_gain_total,
        key_gain_total,
        out_grad,
        ffn_gain_total,
        router_grad,
        gate_grad,
        up_grad,
        down_grad,
    )


def solution(mesh):
    placed = (
        P("fsdp", "ctx", None),
        P(),
        P("fsdp", None),
        P("fsdp", "ctx", None),
        P(),
        P("fsdp", None),
        P("fsdp", None),
        P("fsdp", None),
        P(),
        P(),
        P("fsdp", None),
        P(),
        P("fsdp", None),
        P("ctx", "fsdp", None),
        P("ctx", "fsdp", None),
        P("ctx", "fsdp", None),
        P("fsdp", "ctx", None),
    )
    return jax.shard_map(
        per_device,
        mesh=mesh,
        in_specs=placed,
        out_specs=(
            P("fsdp", "ctx", None),
            P("fsdp", "ctx", None),
            P(),
            P("fsdp", None),
            P("fsdp", None),
            P("fsdp", None),
            P(),
            P(),
            P("fsdp", None),
            P(),
            P("fsdp", None),
            P("ctx", "fsdp", None),
            P("ctx", "fsdp", None),
            P("ctx", "fsdp", None),
        ),
        check_vma=False,
    )
```

profile of v0, /device:TPU:0, one launch (start us, length us, event | category | flops | bytes accessed | tf_op | source)
XLA Modules:
  0.0 2629.6 jit_solution(3409406196270798106)
XLA Ops:
  14.3 43.7 %all-gather.12.cloned.1.call-done = bf16[2048,512]{1,0:T(8,128)(2,1)} async-done(((bf16[512,512]{1,0:T(8,128)(2,1)}), bf16[2048,512]{1,0:T(8,128)(2,1)}) %all-gather.12.cloned.1.call-update) | async-done | bytes 2097168 | tf_op jit(solution)/shard_map/all_gather | solution.py:109
  65.3 38.8 %all-gather.16.cloned.1.call-done = bf16[2048,512]{1,0:T(8,128)(2,1)} async-done(((bf16[512,512]{1,0:T(8,128)(2,1)}), bf16[2048,512]{1,0:T(8,128)(2,1)}) %all-gather.16.cloned.1.call-update) | async-done | bytes 2097168 | tf_op jit(solution)/shard_map/all_gather | solution.py:110
  114.7 13.6 all_gather.42
  135.4 19.2 all-gather.18.cloned.1.call-done
  157.0 285.8 %all-gather.10.cloned.1.call-done = bf16[2048,4096]{1,0:T(8,128)(2,1)} async-done(((bf16[512,4096]{1,0:T(8,128)(2,1)}), bf16[2048,4096]{1,0:T(8,128)(2,1)}) %all-gather.10.cloned.1.call-update) | async-done | bytes 16777232 | tf_op jit(solution)/shard_map/all_gather | solution.py:108
  442.8 23.1 copy.78
  465.9 8.3 multiply_reduce_fusion.3
  481.0 27.0 %while.28 = (s32[]{:T(128)}, bf16[4,8,128,128]{2,3,1,0:T(8,128)(2,1)}, f32[4,8,128]{2,1,0:T(8,128)}, bf16[4,8,128,128]{3,2,1,0:T(8,128)(2,1)S(1)}, bf16[4,1024,1...) while((s32[]{:T(128)}, ...), condition=%wide.region_6.7_spmd.clone, body=%wide.region_3.6_spmd.clone.sunk | while | flops 549846016 | bytes 14462573 | solution.py:158
  508.1 221.2 %all-gather.20.cloned.1.call-done = bf16[4096,2048]{1,0:T(8,128)(2,1)} async-done(((bf16[1024,2048]{1,0:T(8,128)(2,1)}), bf16[4096,2048]{1,0:T(8,128)(2,1)}) %all-gather.20.cloned.1.call-update) | async-done | bytes 16777232 | tf_op jit(solution)/shard_map/all_gather | solution.py:111
  729.2 8.6 multiply_reduce_fusion.8
  747.2 10.7 scatter_custom_fusion.1
  763.4 10.4 scatter_custom_fusion
  773.8 60.4 %all-to-all-done.2 = bf16[8,2,96,2048]{3,2,1,0:T(8,128)(2,1)} async-done(((bf16[8,2,96,2048]{3,2,1,0:T(8,128)(2,1)}), bf16[8,2,96,2048]{3,2,1,0:T(8,128)(2,1)}, u32[]{:S(2)}, u32[]{:S(2)}) %all-to-all-start.2) | async-done | bytes 6291488 | tf_op jit(solution)/shard_map/all_to_all | solution.py:215
  845.6 65.0 %all-to-all-done = bf16[8,2,96,2048]{3,2,1,0:T(8,128)(2,1)} async-done(((bf16[8,2,96,2048]{3,2,1,0:T(8,128)(2,1)}), bf16[8,2,96,2048]{3,2,1,0:T(8,128)(2,1)}, u32[]{:S(2)}, u32[]{:S(2)}) %all-to-all-start) | async-done | bytes 6291488 | tf_op jit(solution)/shard_map/all_to_all | solution.py:190
  917.3 10.4 fusion.103
  927.7 31.8 %all-gather.24.cloned.1.call-done = bf16[2,2048,768]{2,1,0:T(8,128)(2,1)} async-done(((bf16[2,512,768]{2,1,0:T(8,128)(2,1)}), bf16[2,2048,768]{2,1,0:T(8,128)(2,1)}) %all-gather.24.cloned.1.call-update) | async-done | bytes 6291472 | tf_op jit(solution)/shard_map/all_gather | solution.py:168
  959.5 10.4 fusion.104
  969.9 104.8 %all-gather.26.cloned.1.call-done = bf16[2,768,2048]{2,1,0:T(8,128)(2,1)} async-done(((bf16[2,192,2048]{2,1,0:T(8,128)(2,1)}), bf16[2,768,2048]{2,1,0:T(8,128)(2,1)}) %all-gather.26.cloned.1.call-update) | async-done | bytes 6291472 | tf_op jit(solution)/shard_map/all_gather | solution.py:169
  1074.6 13.9 multiply_convert_fusion.1
  1095.4 18.8 copy.93
  1119.4 10.7 fusion.105
  1130.2 10.2 fusion.58
  1140.4 18.8 copy.96
  1159.2 31.8 %all-to-all-done.1 = bf16[1,2,768,2048]{3,1,0,2:T(2,128)(2,1)} async-done(((bf16[1,2,768,2048]{3,1,0,2:T(2,128)(2,1)}), bf16[1,2,768,2048]{3,1,0,2:T(2,128)(2,1)}, u32[]{:S(2)}, u32[]{:S(2)}) %all-to-all-start.1) | async-done | bytes 6291488 | tf_op jit(solution)/shard_map/all_to_all | solution.py:203
  1204.1 12.6 gather_fusion.3
  1224.9 42.5 %all-to-all-done.3 = bf16[1,2,768,2048]{3,1,0,2:T(2,128)(2,1)} async-done(((bf16[1,2,768,2048]{3,1,0,2:T(2,128)(2,1)}), bf16[1,2,768,2048]{3,1,0,2:T(2,128)(2,1)}, u32[]{:S(2)}, u32[]{:S(2)}) %all-to-all-start.3) | async-done | bytes 6291488 | tf_op jit(solution)/shard_map/all_to_all | solution.py:230
  1267.3 8.3 copy.97
  1275.6 12.6 gather_fusion.4
  1298.3 12.7 fusion.72
  1314.0 60.3 %while.29 = (s32[]{:T(128)}, f32[4,8,128,128]{3,2,1,0:T(8,128)}, bf16[4,1024,128]{1,2,0:T(8,128)(2,1)}, bf16[4,1024,128]{1,2,0:T(8,128)(2,1)}, bf16[4,8,128,128]...) while((s32[]{:T(128)}, f32[4,8,128,128]{3,2,1,0:T(8,128)}, ...), condition=%wide.region_20.22_spmd.clone, body=%wide.region_18.21_spmd.clone.sunk | while | flops 1358691328 | bytes 52995752 | solution.py:268
  1379.2 30.1 %reduce-scatter.31.cloned.1.call-done = bf16[128,512]{1,0:T(8,128)(2,1)} async-done(((bf16[1024,512]{1,0:T(8,128)(2,1)}), bf16[128,512]{1,0:T(8,128)(2,1)}) %reduce-scatter.31.cloned.1.call-update) | async-done | bytes 131088
  1412.8 35.6 %reduce-scatter.33.cloned.1.call-done = bf16[128,512]{1,0:T(8,128)(2,1)} async-done(((bf16[1024,512]{1,0:T(8,128)(2,1)}), bf16[128,512]{1,0:T(8,128)(2,1)}) %reduce-scatter.33.cloned.1.call-update) | async-done | bytes 131088
  1451.6 9.4 convolution_convert_fusion
  1468.7 11.7 convolution_convert_fusion.1
  1482.5 9.7 convolution_convert_fusion.3
  1492.2 9.7 convolution_convert_fusion.5
  1502.0 9.9 convolution_convert_fusion.4
  1512.0 27.4 %reduce-scatter.19.cloned.1.call-done = bf16[512,512]{1,0:T(8,128)(2,1)} async-done(((bf16[2048,512]{1,0:T(8,128)(2,1)}), bf16[512,512]{1,0:T(8,128)(2,1)}) %reduce-scatter.19.cloned.1.call-update) | async-done | bytes 524304 | tf_op jit(solution)/shard_map/reduce_scatter | solution.py:327
  1539.4 281.9 %reduce-scatter.21.cloned.1.call-done = bf16[1024,2048]{1,0:T(8,128)(2,1)} async-done(((bf16[4096,2048]{1,0:T(8,128)(2,1)}), bf16[1024,2048]{1,0:T(8,128)(2,1)}) %reduce-scatter.21.cloned.1.call-update) | async-done | bytes 4194320 | tf_op jit(solution)/shard_map/reduce_scatter | solution.py:330
  1821.3 283.3 %reduce-scatter.15.cloned.1.call-done = bf16[512,4096]{1,0:T(8,128)(2,1)} async-done(((bf16[2048,4096]{1,0:T(8,128)(2,1)}), bf16[512,4096]{1,0:T(8,128)(2,1)}) %reduce-scatter.15.cloned.1.call-update) | async-done | bytes 4194320 | tf_op jit(solution)/shard_map/reduce_scatter | solution.py:321
  2105.8 11.5 fusion.106
  2117.4 9.8 reduce-scatter.23.cloned.1.call-done
  2127.2 23.7 psum.71
  2155.1 42.7 %all-reduce = (f32[2048]{0:T(1024)}, f32[128]{0:T(128)}, f32[128]{0:T(128)}, f32[2048]{0:T(1024)}) all-reduce(f32[2048]{0:T(1024)S(1)} %get-tuple-element.220, f32[128]{0:T(128)S(1)} %get-tuple-element.216, f32[128]{0:T(128)S(1)} %get-tuple-element.222, f32[2048]{0:T(1024)S(1)} %copy-done.57), channel_id=1, replica_groups=mesh['ctx'=8,'fsdp'=4] {'ctx','fsdp'}, use_global_device_ids=true, to_apply=%region_27.29 | all-reduce | flops 4352 | bytes 34816 | tf_op jit(solution)/shard_map/psum | solution.py:344
  2199.1 40.3 %reduce-scatter.29.cloned.1.call-done = bf16[2,192,2048]{2,1,0:T(8,128)(2,1)} async-done(((bf16[2,768,2048]{2,1,0:T(8,128)(2,1)}), bf16[2,192,2048]{2,1,0:T(8,128)(2,1)}) %reduce-scatter.29.cloned.1.call-update) | async-done | bytes 1572880 | tf_op jit(solution)/shard_map/reduce_scatter | solution.py:316
  2242.8 110.6 %reduce-scatter.25.cloned.1.call-done = bf16[2,512,768]{2,1,0:T(8,128)(2,1)} async-done(((bf16[2,2048,768]{2,1,0:T(8,128)(2,1)}), bf16[2,512,768]{2,1,0:T(8,128)(2,1)}) %reduce-scatter.25.cloned.1.call-update) | async-done | bytes 1572880 | tf_op jit(solution)/shard_map/reduce_scatter | solution.py:310
  2356.7 110.3 %reduce-scatter.27.cloned.1.call-done = bf16[2,512,768]{2,1,0:T(8,128)(2,1)} async-done(((bf16[2,2048,768]{2,1,0:T(8,128)(2,1)}), bf16[2,512,768]{2,1,0:T(8,128)(2,1)}) %reduce-scatter.27.cloned.1.call-update) | async-done | bytes 1572880 | tf_op jit(solution)/shard_map/reduce_scatter | solution.py:313
  2470.3 138.7 %all-reduce.4.cloned.1.call-done = (bf16[512,4096]{1,0:T(8,128)(2,1)}, bf16[512,512]{1,0:T(8,128)(2,1)}, bf16[512,512]{1,0:T(8,128)(2,1)}, bf16[1024,2048]{1,0:T(8,128)(2,1)}) async-done(((bf16[512,4096]{1,0:T(8,128)(2,1)}, bf16[512,512]{1,0:T(8,128)(2,1)}, bf16[512,512]{1,0:T(8,128)(2,1)}, bf16[1024,2048]{1,0:T(8,128)(2,1)}), (bf16[512,4096]{1,0:T(8,128)(2,1)}, bf16[512,512]{1,0:T(8,128)(2,1)}, ...) | async-done | bytes 9437200 | tf_op jit(solution)/shard_map/psum | solution.py:338
  (370 shorter events, 258.0 us)
Async XLA Ops:
  7.2 50.8 %all-gather.12.cloned.1.call-start = ((), (), s32[]{:S(2)}) async-start(), calls=%async_computation.15 | async-start | bytes 2621440 | tf_op jit(solution)/shard_map/all_gather | solution.py:109
  7.9 96.1 %all-gather.16.cloned.1.call-start = ((), (), s32[]{:S(2)}) async-start(), calls=%async_computation.17 | async-start | bytes 2621440 | tf_op jit(solution)/shard_map/all_gather | solution.py:110
  8.7 125.1 %all-gather.14.cloned.1.call-start = ((), (), s32[]{:S(2)}) async-start(), calls=%async_computation.16 | async-start | bytes 1179648 | tf_op jit(solution)/shard_map/all_gather | solution.py:127
  12.1 91.9 %copy-start.59 = (f32[128]{0:T(128)}, f32[128]{0:T(128)S(1)}, u32[]{:S(2)}) copy-start(f32[128]{0:T(128)S(1)} %add_rsqrt_fusion.3) | copy-start | bytes 1540
  12.9 463.0 %copy-start.29 = (f32[128,64]{0,1:T(8,128)}, f32[128,64]{0,1:T(8,128)S(1)}, u32[]{:S(2)}) copy-start(f32[128,64]{0,1:T(8,128)S(1)} %get-tuple-element.297) | copy-start | bytes 98308
  12.9 463.0 %copy-start.31 = (f32[128,64]{0,1:T(8,128)}, f32[128,64]{0,1:T(8,128)S(1)}, u32[]{:S(2)}) copy-start(f32[128,64]{0,1:T(8,128)S(1)} %get-tuple-element.298) | copy-start | bytes 98308
  12.9 51.5 %copy-start.61 = (f32[128]{0:T(128)S(1)}, f32[128]{0:T(128)}, u32[]{:S(2)}) copy-start(f32[128]{0:T(128)} %param.32) | copy-start | bytes 1540
  14.3 451.6 %copy-start.13 = (bf16[1,128,2048]{2,1,0:T(8,128)(2,1)}, bf16[1,128,2048]{2,1,0:T(8,128)(2,1)S(1)}, u32[]{:S(2)}) copy-start(bf16[1,128,2048]{2,1,0:T(8,128)(2,1)S(1)} %multiply_convert_fusion.7) | copy-start | bytes 1572868
  58.0 46.1 %copy-start.3 = (f32[1,128,2048]{2,1,0:T(8,128)S(1)}, f32[1,128,2048]{2,1,0:T(8,128)}, u32[]{:S(2)}) copy-start(f32[1,128,2048]{2,1,0:T(8,128)} %param.23) | copy-start | bytes 3145732
  58.0 46.1 %copy-start.46 = (f32[2048]{0:T(1024)S(1)}, f32[2048]{0:T(1024)}, u32[]{:S(2)}) copy-start(f32[2048]{0:T(1024)} %param.27) | copy-start | bytes 24580
  64.3 43.1 %copy-start.23 = (f32[128,4,128]{0,2,1:T(8,128)}, f32[128,4,128]{0,2,1:T(8,128)S(1)}, u32[]{:S(2)}) copy-start(f32[128,4,128]{0,2,1:T(8,128)S(1)} %get-tuple-element.304) | copy-start | bytes 786436
  64.4 43.1 %copy-start.55 = (f32[128,4]{0,1:T(4,128)}, f32[128,4]{0,1:T(4,128)S(1)}, u32[]{:S(2)}) copy-start(f32[128,4]{0,1:T(4,128)S(1)} %add_rsqrt_fusion.1) | copy-start | bytes 6148
  65.2 89.4 %all-gather.18.cloned.1.call-start = ((), (), s32[]{:S(2)}) async-start(), calls=%async_computation.18 | async-start | bytes 1179648 | tf_op jit(solution)/shard_map/all_gather | solution.py:128
  106.9 336.0 %all-gather.10.cloned.1.call-start = ((), (), s32[]{:S(2)}) async-start(), calls=%async_computation.14 | async-start | bytes 20971520 | tf_op jit(solution)/shard_map/all_gather | solution.py:108
  107.5 621.7 %all-gather.20.cloned.1.call-start = ((), (), s32[]{:S(2)}) async-start(), calls=%async_computation.19 | async-start | bytes 20971520 | tf_op jit(solution)/shard_map/all_gather | solution.py:111
  108.1 809.2 %all-gather.22.cloned.1.call-start = ((), (), s32[]{:S(2)}) async-start(), calls=%async_computation.20 | async-start | bytes 7864320 | tf_op jit(solution)/shard_map/all_gather | solution.py:167
  108.8 850.7 %all-gather.24.cloned.1.call-start = ((), (), s32[]{:S(2)}) async-start(), calls=%async_computation.21 | async-start | bytes 7864320 | tf_op jit(solution)/shard_map/all_gather | solution.py:168
  128.3 610.7 %copy-start.33 = (bf16[2048,16]{0,1:T(8,128)(2,1)}, bf16[2048,16]{0,1:T(8,128)(2,1)S(1)}, u32[]{:S(2)}) copy-start(bf16[2048,16]{0,1:T(8,128)(2,1)S(1)} %all_gather.42) | copy-start | bytes 196612
  133.7 332.2 %copy-start.50 = (s32[1024]{0:T(1024)}, s32[1024]{0:T(1024)S(1)}, u32[]{:S(2)}) copy-start(s32[1024]{0:T(1024)S(1)} %fusion.88) | copy-start | bytes 12292
  508.0 229.7 %copy-start.7 = (bf16[4,1024,128]{2,1,0:T(8,128)(2,1)}, bf16[4,1024,128]{2,1,0:T(8,128)(2,1)S(1)}, u32[]{:S(2)}) copy-start(bf16[4,1024,128]{2,1,0:T(8,128)(2,1)S(1)} %get-tuple-element.573) | copy-start | bytes 3145732
  508.0 229.7 %copy-start.15 = (bf16[4,8,128,128]{3,2,1,0:T(8,128)(2,1)}, bf16[4,8,128,128]{3,2,1,0:T(8,128)(2,1)S(1)}, u32[]{:S(2)}) copy-start(bf16[4,8,128,128]{3,2,1,0:T(8,128)(2,1)S(1)} %get-tuple-element.574) | copy-start | bytes 3145732
  508.0 229.8 %copy-start.35 = (s32[1024]{0:T(1024)}, s32[1024]{0:T(1024)S(1)}, u32[]{:S(2)}) copy-start(s32[1024]{0:T(1024)S(1)} %get-tuple-element.615) | copy-start | bytes 12292
  508.0 229.8 %copy-start.40 = (s32[1024]{0:T(1024)}, s32[1024]{0:T(1024)S(1)}, u32[]{:S(2)}) copy-start(s32[1024]{0:T(1024)S(1)} %get-tuple-element.631) | copy-start | bytes 12292
  508.0 229.8 %copy-start.52 = (s32[128]{0:T(128)}, s32[128]{0:T(128)S(1)}, u32[]{:S(2)}) copy-start(s32[128]{0:T(128)S(1)} %get-tuple-element.635) | copy-start | bytes 1540
  757.9 76.3 %all-to-all-start.2 = ((bf16[8,2,96,2048]{3,2,1,0:T(8,128)(2,1)}), bf16[8,2,96,2048]{3,2,1,0:T(8,128)(2,1)}, u32[]{:S(2)}, u32[]{:S(2)}) async-start(bf16[8,2,96,2048]{3,2,1,0:T(8,128)(2,1)} %bitcast.321), calls=%async_computation.2 | async-start | bytes 12582912 | tf_op jit(solution)/shard_map/all_to_all | solution.py:215
  762.7 312.0 %all-gather.26.cloned.1.call-start = ((), (), s32[]{:S(2)}) async-start(), calls=%async_computation.22 | async-start | bytes 7864320 | tf_op jit(solution)/shard_map/all_gather | solution.py:169
  834.2 76.4 %all-to-all-start = ((bf16[8,2,96,2048]{3,2,1,0:T(8,128)(2,1)}), bf16[8,2,96,2048]{3,2,1,0:T(8,128)(2,1)}, u32[]{:S(2)}, u32[]{:S(2)}) async-start(bf16[8,2,96,2048]{3,2,1,0:T(8,128)(2,1)} %bitcast.322), calls=%async_computation | async-start | bytes 12582912 | tf_op jit(solution)/shard_map/all_to_all | solution.py:190
  1114.2 76.8 %all-to-all-start.1 = ((bf16[1,2,768,2048]{3,1,0,2:T(2,128)(2,1)}), bf16[1,2,768,2048]{3,1,0,2:T(2,128)(2,1)}, u32[]{:S(2)}, u32[]{:S(2)}) async-start(bf16[1,2,768,2048]{3,1,0,2:T(2,128)(2,1)} %copy.93), calls=%async_computation.1 | async-start | bytes 12582912 | tf_op jit(solution)/shard_map/all_to_all | solution.py:203
  1159.2 36.7 %copy-start.51 = (s32[1024]{0:T(1024)S(1)}, s32[1024]{0:T(1024)}, u32[]{:S(2)}) copy-start(s32[1024]{0:T(1024)} %copy-done.50) | copy-start | bytes 12292
  1191.0 76.3 %all-to-all-start.3 = ((bf16[1,2,768,2048]{3,1,0,2:T(2,128)(2,1)}), bf16[1,2,768,2048]{3,1,0,2:T(2,128)(2,1)}, u32[]{:S(2)}, u32[]{:S(2)}) async-start(bf16[1,2,768,2048]{3,1,0,2:T(2,128)(2,1)} %copy.96), calls=%async_computation.3 | async-start | bytes 12582912 | tf_op jit(solution)/shard_map/all_to_all | solution.py:230
  1195.7 213.5 %reduce-scatter.31.cloned.1.call-start = ((), (), s32[]{:S(2)}) async-start(), calls=%async_computation.31 | async-start | bytes 1179648
  1298.3 153.3 %copy-start.9 = (f32[128,2048]{1,0:T(8,128)}, f32[128,2048]{1,0:T(8,128)S(1)}, u32[]{:S(2)}) copy-start(f32[128,2048]{1,0:T(8,128)S(1)} %get-tuple-element.291) | copy-start | bytes 3145732
  1374.4 36.3 %copy-start.14 = (bf16[1,128,2048]{2,1,0:T(8,128)(2,1)S(1)}, bf16[1,128,2048]{2,1,0:T(8,128)(2,1)}, u32[]{:S(2)}) copy-start(bf16[1,128,2048]{2,1,0:T(8,128)(2,1)} %copy-done.13) | copy-start | bytes 1572868
  1376.7 71.7 %reduce-scatter.33.cloned.1.call-start = ((), (), s32[]{:S(2)}) async-start(), calls=%async_computation.32 | async-start | bytes 1179648
  1379.1 69.3 %copy-start.4 = (f32[1,128,2048]{2,1,0:T(8,128)S(1)}, f32[1,128,2048]{2,1,0:T(8,128)}, u32[]{:S(2)}) copy-start(f32[1,128,2048]{2,1,0:T(8,128)} %param.23) | copy-start | bytes 3145732
  1379.1 69.3 %copy-start.47 = (f32[2048]{0:T(1024)S(1)}, f32[2048]{0:T(1024)}, u32[]{:S(2)}) copy-start(f32[2048]{0:T(1024)} %param.27) | copy-start | bytes 24580
  1379.1 69.3 %copy-start.60 = (f32[128]{0:T(128)S(1)}, f32[128]{0:T(128)}, u32[]{:S(2)}) copy-start(f32[128]{0:T(128)} %copy-done.59) | copy-start | bytes 1540
  1379.1 132.9 %reduce-scatter.17.cloned.1.call-start = ((), (), s32[]{:S(2)}) async-start(), calls=%async_computation.24 | async-start | bytes 2621440 | tf_op jit(solution)/shard_map/reduce_scatter | solution.py:324
  1412.8 126.6 %reduce-scatter.19.cloned.1.call-start = ((), (), s32[]{:S(2)}) async-start(), calls=%async_computation.25 | async-start | bytes 2621440 | tf_op jit(solution)/shard_map/reduce_scatter | solution.py:327
  1451.5 369.8 %reduce-scatter.21.cloned.1.call-start = ((), (), s32[]{:S(2)}) async-start(), calls=%async_computation.26 | async-start | bytes 20971520 | tf_op jit(solution)/shard_map/reduce_scatter | solution.py:330
  1461.0 643.6 %reduce-scatter.15.cloned.1.call-start = ((), (), s32[]{:S(2)}) async-start(), calls=%async_computation.23 | async-start | bytes 20971520 | tf_op jit(solution)/shard_map/reduce_scatter | solution.py:321
  1480.5 646.7 %reduce-scatter.23.cloned.1.call-start = ((), (), s32[]{:S(2)}) async-start(), calls=%async_computation.27 | async-start | bytes 81920 | tf_op jit(solution)/shard_map/reduce_scatter | solution.py:333
  1482.4 757.0 %reduce-scatter.29.cloned.1.call-start = ((), (), s32[]{:S(2)}) async-start(), calls=%async_computation.30 | async-start | bytes 7864320 | tf_op jit(solution)/shard_map/reduce_scatter | solution.py:316
  1492.2 861.2 %reduce-scatter.25.cloned.1.call-start = ((), (), s32[]{:S(2)}) async-start(), calls=%async_computation.28 | async-start | bytes 7864320 | tf_op jit(solution)/shard_map/reduce_scatter | solution.py:310
  1502.0 965.1 %reduce-scatter.27.cloned.1.call-start = ((), (), s32[]{:S(2)}) async-start(), calls=%async_computation.29 | async-start | bytes 7864320 | tf_op jit(solution)/shard_map/reduce_scatter | solution.py:313
  1511.9 1097.1 %all-reduce.4.cloned.1.call-start = ((), (), s32[]{:S(2)}) async-start(), calls=%async_computation.33 | async-start | bytes 18874368 | tf_op jit(solution)/shard_map/psum | solution.py:338
  2117.4 36.8 %copy-start.39 = (bf16[128,512]{1,0:T(8,128)(2,1)S(1)}, bf16[128,512]{1,0:T(8,128)(2,1)}, u32[]{:S(2)}) copy-start(bf16[128,512]{1,0:T(8,128)(2,1)} %reduce-scatter.33.cloned.1.call-done) | copy-start | bytes 393220
  2151.6 46.2 %copy-start.10 = (f32[128,2048]{1,0:T(8,128)S(1)}, f32[128,2048]{1,0:T(8,128)}, u32[]{:S(2)}) copy-start(f32[128,2048]{1,0:T(8,128)} %copy-done.9) | copy-start | bytes 3145732
  (49 other events, 431.6 us)
Sparse Core Ops, SparseCore 0:
  9.6 48.3 all-gather.11
  59.6 44.4 all-gather.15
  106.5 22.2 all-gather.13
  131.1 23.4 all-gather.17
  156.0 286.7 all-gather.9
  444.2 284.9 all-gather.19
  730.8 113.5 all-gather.21
  845.9 113.5 all-gather.23
  961.1 113.5 all-gather.25
  1376.9 32.3 reduce-scatter.30
  1412.4 35.9 reduce-scatter.32
  1450.6 43.6 reduce-scatter.16
  1496.5 42.8 reduce-scatter.18
  1541.6 279.6 reduce-scatter.20
  1823.5 281.0 reduce-scatter.14
  2107.3 19.9 reduce-scatter.22
  2129.4 109.9 reduce-scatter.28
  2242.1 111.2 reduce-scatter.24
  2355.7 111.2 reduce-scatter.26
  2470.8 138.1 all-reduce.3
where the time goes:
time: 2640 us; the launch traced here: 2630 us
  waiting for transfers between devices  2020 us (77%)
  matrix products  236 us (9%)
  local copies, waits for them, and re-layouts  178 us (7%)
  other arithmetic  81.3 us (3%)
  blocking collectives  80 us (3%)
    all_gather x1, waiting for transfers between devices, per_device(): lax.all_gather(query_proj, 'fsdp', axis=0, tiled=True)  286 us
    reduce_scatter x1, waiting for transfers between devices, per_device(): lax.psum_scatter(query_grad_full.astype(jnp.bfloat16), 'fsdp', scatter_di...  283 us
    reduce_scatter x1, waiting for transfers between devices, per_device(): lax.psum_scatter(out_grad_full.astype(jnp.bfloat16), 'fsdp', scatter_dime...  282 us
    all_gather x1, waiting for transfers between devices, per_device(): lax.all_gather(out_proj, 'fsdp', axis=0, tiled=True)  221 us
    dot_general x47, matrix products, contract(): return jnp.einsum(form, left, right, preferred_element_type=jnp.float32)  206 us
    psum x1, waiting for transfers between devices, per_device(): lax.psum(shard_grads[0].astype(jnp.bfloat16), 'ctx').astype(jnp.float32)  139 us
    reduce_scatter x1, waiting for transfers between devices, per_device(): lax.psum_scatter(gate_grad_full.astype(jnp.bfloat16), 'fsdp', scatter_dim...  111 us
    reduce_scatter x1, waiting for transfers between devices, per_device(): lax.psum_scatter(up_grad_full.astype(jnp.bfloat16), 'fsdp', scatter_dimen...  110 us
  transfers between devices with their start and end apart: 24, of which 21 were waited for; matrix products, arithmetic and copies ran while one was open for 13% of the time, Pallas kernels for 0%

commit v1 on v0

--- a/solution.py
+++ b/solution.py
@@ -2,6 +2,7 @@
 import jax.numpy as jnp
 from jax import lax
 from jax.sharding import PartitionSpec as P
+from jax.lax import all_gather
 
 D = 2048
 HEADS = 32
@@ -335,7 +336,7 @@
         ).astype(jnp.float32),
     )
     query_grad, key_grad, value_grad, out_grad, router_grad = (
-        lax.psum(shard_grads[0].astype(jnp.bfloat16), "ctx").astype(jnp.float32),
+        jnp.sum(all_gather(shard_grads[0].astype(jnp.bfloat16), "ctx"), 0).astype(jnp.float32),
         lax.psum(shard_grads[1].astype(jnp.bfloat16), "ctx").astype(jnp.float32),
         lax.psum(shard_grads[2].astype(jnp.bfloat16), "ctx").astype(jnp.float32),
         lax.psum(shard_grads[3].astype(jnp.bfloat16), "ctx").astype(jnp.float32),

time: 2640 us -> 2760 us (1.045)
  waiting for transfers between devices: 2020 us -> 2130 us
    all_gather x0 -> x1, waiting for transfers between devices: none -> 154 us  [per_device(): all_gather(shard_grads[0].astype(jnp.bfloat16), 'ctx')]
    psum x1, waiting for transfers between devices: 139 us -> 93 us  [per_device(): lax.psum(shard_grads[1].astype(jnp.bfloat16), 'ctx').astype(jnp.float32)]
    unnamed x22 -> x23, waiting for transfers between devices: 70.4 us -> 70.4 us
  transfers between devices with their start and end apart: 24 -> 25, of which waited for: 21 -> 22; matrix products, arithmetic and copies ran while one was open for 13% -> 12% of each run, Pallas kernels for 0% -> 0%
where the time goes in v1:
time: 2760 us; the launch traced here: 2750 us
  waiting for transfers between devices  2130 us (77%)
  matrix products  236 us (9%)
  local copies, waits for them, and re-layouts  177 us (6%)
  other arithmetic  98 us (4%)
  blocking collectives  80 us (3%)
    all_gather x1, waiting for transfers between devices, per_device(): lax.all_gather(query_proj, 'fsdp', axis=0, tiled=True)  286 us
    reduce_scatter x1, waiting for transfers between devices, per_device(): lax.psum_scatter(query_grad_full.astype(jnp.bfloat16), 'fsdp', scatter_di...  283 us
    reduce_scatter x1, waiting for transfers between devices, per_device(): lax.psum_scatter(out_grad_full.astype(jnp.bfloat16), 'fsdp', scatter_dime...  282 us
    all_gather x1, waiting for transfers between devices, per_device(): lax.all_gather(out_proj, 'fsdp', axis=0, tiled=True)  221 us
    dot_general x47, matrix products, contract(): return jnp.einsum(form, left, right, preferred_element_type=jnp.float32)  206 us
    all_gather x1, waiting for transfers between devices, per_device(): all_gather(shard_grads[0].astype(jnp.bfloat16), 'ctx')  154 us
    reduce_scatter x1, waiting for transfers between devices, per_device(): lax.psum_scatter(gate_grad_full.astype(jnp.bfloat16), 'fsdp', scatter_dim...  111 us
    reduce_scatter x1, waiting for transfers between devices, per_device(): lax.psum_scatter(up_grad_full.astype(jnp.bfloat16), 'fsdp', scatter_dimen...  110 us
  transfers between devices with their start and end apart: 25, of which 22 were waited for; matrix products, arithmetic and copies ran while one was open for 12% of the time, Pallas kernels for 0%

profile of v1, /device:TPU:0, one launch (start us, length us, event | category | flops | bytes accessed | tf_op | source)
XLA Modules:
  0.0 2754.2 jit_solution(14238966790512579599)
XLA Ops:
  14.3 43.6 %all-gather.14.cloned.1.call-done = bf16[2048,512]{1,0:T(8,128)(2,1)} async-done(((bf16[512,512]{1,0:T(8,128)(2,1)}), bf16[2048,512]{1,0:T(8,128)(2,1)}) %all-gather.14.cloned.1.call-update) | async-done | bytes 2097168 | tf_op jit(solution)/shard_map/all_gather | solution.py:110
  65.3 38.8 %all-gather.18.cloned.1.call-done = bf16[2048,512]{1,0:T(8,128)(2,1)} async-done(((bf16[512,512]{1,0:T(8,128)(2,1)}), bf16[2048,512]{1,0:T(8,128)(2,1)}) %all-gather.18.cloned.1.call-update) | async-done | bytes 2097168 | tf_op jit(solution)/shard_map/all_gather | solution.py:111
  114.7 13.7 all_gather.48
  135.5 19.1 all-gather.20.cloned.1.call-done
  156.9 285.8 %all-gather.12.cloned.1.call-done = bf16[2048,4096]{1,0:T(8,128)(2,1)} async-done(((bf16[512,4096]{1,0:T(8,128)(2,1)}), bf16[2048,4096]{1,0:T(8,128)(2,1)}) %all-gather.12.cloned.1.call-update) | async-done | bytes 16777232 | tf_op jit(solution)/shard_map/all_gather | solution.py:109
  442.7 23.1 copy.78
  480.9 27.2 while.28
  508.1 221.0 %all-gather.22.cloned.1.call-done = bf16[4096,2048]{1,0:T(8,128)(2,1)} async-done(((bf16[1024,2048]{1,0:T(8,128)(2,1)}), bf16[4096,2048]{1,0:T(8,128)(2,1)}) %all-gather.22.cloned.1.call-update) | async-done | bytes 16777232 | tf_op jit(solution)/shard_map/all_gather | solution.py:112
  729.2 8.6 multiply_reduce_fusion.8
  747.2 10.7 scatter_custom_fusion.1
  763.3 10.4 scatter_custom_fusion
  773.8 60.4 %all-to-all-done.2 = bf16[8,2,96,2048]{3,2,1,0:T(8,128)(2,1)} async-done(((bf16[8,2,96,2048]{3,2,1,0:T(8,128)(2,1)}), bf16[8,2,96,2048]{3,2,1,0:T(8,128)(2,1)}, u32[]{:S(2)}, u32[]{:S(2)}) %all-to-all-start.2) | async-done | bytes 6291488 | tf_op jit(solution)/shard_map/all_to_all | solution.py:216
  845.6 65.0 %all-to-all-done = bf16[8,2,96,2048]{3,2,1,0:T(8,128)(2,1)} async-done(((bf16[8,2,96,2048]{3,2,1,0:T(8,128)(2,1)}), bf16[8,2,96,2048]{3,2,1,0:T(8,128)(2,1)}, u32[]{:S(2)}, u32[]{:S(2)}) %all-to-all-start) | async-done | bytes 6291488 | tf_op jit(solution)/shard_map/all_to_all | solution.py:191
  917.2 10.5 fusion.103
  927.7 31.7 %all-gather.26.cloned.1.call-done = bf16[2,2048,768]{2,1,0:T(8,128)(2,1)} async-done(((bf16[2,512,768]{2,1,0:T(8,128)(2,1)}), bf16[2,2048,768]{2,1,0:T(8,128)(2,1)}) %all-gather.26.cloned.1.call-update) | async-done | bytes 6291472 | tf_op jit(solution)/shard_map/all_gather | solution.py:169
  959.4 10.3 fusion.104
  969.8 104.8 %all-gather.28.cloned.1.call-done = bf16[2,768,2048]{2,1,0:T(8,128)(2,1)} async-done(((bf16[2,192,2048]{2,1,0:T(8,128)(2,1)}), bf16[2,768,2048]{2,1,0:T(8,128)(2,1)}) %all-gather.28.cloned.1.call-update) | async-done | bytes 6291472 | tf_op jit(solution)/shard_map/all_gather | solution.py:170
  1074.6 13.9 multiply_convert_fusion.1
  1095.3 18.8 copy.93
  1119.4 10.7 fusion.105
  1130.1 10.2 fusion.58
  1140.3 18.8 copy.96
  1159.1 31.8 %all-to-all-done.1 = bf16[1,2,768,2048]{3,1,0,2:T(2,128)(2,1)} async-done(((bf16[1,2,768,2048]{3,1,0,2:T(2,128)(2,1)}), bf16[1,2,768,2048]{3,1,0,2:T(2,128)(2,1)}, u32[]{:S(2)}, u32[]{:S(2)}) %all-to-all-start.1) | async-done | bytes 6291488 | tf_op jit(solution)/shard_map/all_to_all | solution.py:204
  1204.2 12.6 gather_fusion.3
  1224.8 42.4 %all-to-all-done.3 = bf16[1,2,768,2048]{3,1,0,2:T(2,128)(2,1)} async-done(((bf16[1,2,768,2048]{3,1,0,2:T(2,128)(2,1)}), bf16[1,2,768,2048]{3,1,0,2:T(2,128)(2,1)}, u32[]{:S(2)}, u32[]{:S(2)}) %all-to-all-start.3) | async-done | bytes 6291488 | tf_op jit(solution)/shard_map/all_to_all | solution.py:231
  1275.6 12.6 gather_fusion.4
  1298.3 12.7 fusion.72
  1314.0 60.4 %while.29 = (s32[]{:T(128)}, f32[4,8,128,128]{3,2,1,0:T(8,128)}, bf16[4,1024,128]{1,2,0:T(8,128)(2,1)}, bf16[4,1024,128]{1,2,0:T(8,128)(2,1)}, bf16[4,8,128,128]...) while((s32[]{:T(128)}, f32[4,8,128,128]{3,2,1,0:T(8,128)}, ...), condition=%wide.region_20.22_spmd.clone, body=%wide.region_18.21_spmd.clone.sunk | while | flops 1358691328 | bytes 52995752 | solution.py:269
  1379.3 30.1 %reduce-scatter.31.cloned.1.call-done = bf16[128,512]{1,0:T(8,128)(2,1)} async-done(((bf16[1024,512]{1,0:T(8,128)(2,1)}), bf16[128,512]{1,0:T(8,128)(2,1)}) %reduce-scatter.31.cloned.1.call-update) | async-done | bytes 131088
  1413.0 35.6 %reduce-scatter.33.cloned.1.call-done = bf16[128,512]{1,0:T(8,128)(2,1)} async-done(((bf16[1024,512]{1,0:T(8,128)(2,1)}), bf16[128,512]{1,0:T(8,128)(2,1)}) %reduce-scatter.33.cloned.1.call-update) | async-done | bytes 131088
  1451.7 9.3 convolution_convert_fusion
  1468.8 11.7 convolution_convert_fusion.1
  1482.5 9.7 convolution_convert_fusion.3
  1492.2 9.7 convolution_convert_fusion.5
  1502.0 9.9 convolution_convert_fusion.4
  1512.0 27.5 reduce-scatter.19.cloned.1.call-done
  1539.5 281.9 %reduce-scatter.21.cloned.1.call-done = bf16[1024,2048]{1,0:T(8,128)(2,1)} async-done(((bf16[4096,2048]{1,0:T(8,128)(2,1)}), bf16[1024,2048]{1,0:T(8,128)(2,1)}) %reduce-scatter.21.cloned.1.call-update) | async-done | bytes 4194320 | tf_op jit(solution)/shard_map/reduce_scatter | solution.py:331
  1821.5 283.2 %reduce-scatter.15.cloned.1.call-done = bf16[512,4096]{1,0:T(8,128)(2,1)} async-done(((bf16[2048,4096]{1,0:T(8,128)(2,1)}), bf16[512,4096]{1,0:T(8,128)(2,1)}) %reduce-scatter.15.cloned.1.call-update) | async-done | bytes 4194320 | tf_op jit(solution)/shard_map/reduce_scatter | solution.py:322
  2104.8 11.5 fusion.106
  2116.3 11.0 reduce-scatter.23.cloned.1.call-done
  2127.3 23.7 psum.63
  2155.3 42.6 %all-reduce = (f32[2048]{0:T(1024)}, f32[128]{0:T(128)}, f32[128]{0:T(128)}, f32[2048]{0:T(1024)}) all-reduce(f32[2048]{0:T(1024)S(1)} %get-tuple-element.220, f32[128]{0:T(128)S(1)} %get-tuple-element.216, f32[128]{0:T(128)S(1)} %get-tuple-element.222, f32[2048]{0:T(1024)S(1)} %copy-done.56), channel_id=1, replica_groups=mesh['ctx'=8,'fsdp'=4] {'ctx','fsdp'}, use_global_device_ids=true, to_apply=%region_27.29 | all-reduce | flops 4352 | bytes 34816 | tf_op jit(solution)/shard_map/psum | solution.py:345
  2199.2 40.3 %reduce-scatter.29.cloned.1.call-done = bf16[2,192,2048]{2,1,0:T(8,128)(2,1)} async-done(((bf16[2,768,2048]{2,1,0:T(8,128)(2,1)}), bf16[2,192,2048]{2,1,0:T(8,128)(2,1)}) %reduce-scatter.29.cloned.1.call-update) | async-done | bytes 1572880 | tf_op jit(solution)/shard_map/reduce_scatter | solution.py:317
  2242.9 110.6 %reduce-scatter.25.cloned.1.call-done = bf16[2,512,768]{2,1,0:T(8,128)(2,1)} async-done(((bf16[2,2048,768]{2,1,0:T(8,128)(2,1)}), bf16[2,512,768]{2,1,0:T(8,128)(2,1)}) %reduce-scatter.25.cloned.1.call-update) | async-done | bytes 1572880 | tf_op jit(solution)/shard_map/reduce_scatter | solution.py:311
  2356.8 110.3 %reduce-scatter.27.cloned.1.call-done = bf16[2,512,768]{2,1,0:T(8,128)(2,1)} async-done(((bf16[2,2048,768]{2,1,0:T(8,128)(2,1)}), bf16[2,512,768]{2,1,0:T(8,128)(2,1)}) %reduce-scatter.27.cloned.1.call-update) | async-done | bytes 1572880 | tf_op jit(solution)/shard_map/reduce_scatter | solution.py:314
  2470.4 93.0 %all-reduce.4.cloned.1.call-done = (bf16[512,512]{1,0:T(8,128)(2,1)}, bf16[512,512]{1,0:T(8,128)(2,1)}, bf16[1024,2048]{1,0:T(8,128)(2,1)}) async-done(((bf16[512,512]{1,0:T(8,128)(2,1)}, bf16[512,512]{1,0:T(8,128)(2,1)}, bf16[1024,2048]{1,0:T(8,128)(2,1)}), (bf16[512,512]{1,0:T(8,128)(2,1)}, bf16[512,512]{1,0:T(8,128)(2,1)}, bf16[1024,2048]{1,0:T(8,128)(2,1)})) %all-reduce.4.cloned.1.call-update) | async-done | bytes 5242896 | tf_op jit(solution)/shard_map/psum | solution.py:340
  2572.4 153.7 %all-gather.30.cloned.1.call-done = bf16[4096,4096]{1,0:T(8,128)(2,1)} async-done(((bf16[512,4096]{1,0:T(8,128)(2,1)}), bf16[4096,4096]{1,0:T(8,128)(2,1)}) %all-gather.30.cloned.1.call-update) | async-done | bytes 33554448 | tf_op jit(solution)/shard_map/all_gather | solution.py:339
  2726.2 14.2 reduce_sum.190
  (372 shorter events, 276.0 us)
Async XLA Ops:
  7.2 50.8 %all-gather.14.cloned.1.call-start = ((), (), s32[]{:S(2)}) async-start(), calls=%async_computation.15 | async-start | bytes 2621440 | tf_op jit(solution)/shard_map/all_gather | solution.py:110
  7.9 96.1 %all-gather.18.cloned.1.call-start = ((), (), s32[]{:S(2)}) async-start(), calls=%async_computation.17 | async-start | bytes 2621440 | tf_op jit(solution)/shard_map/all_gather | solution.py:111
  8.7 125.1 %all-gather.16.cloned.1.call-start = ((), (), s32[]{:S(2)}) async-start(), calls=%async_computation.16 | async-start | bytes 1179648 | tf_op jit(solution)/shard_map/all_gather | solution.py:128
  12.1 91.9 %copy-start.58 = (f32[128]{0:T(128)}, f32[128]{0:T(128)S(1)}, u32[]{:S(2)}) copy-start(f32[128]{0:T(128)S(1)} %add_rsqrt_fusion.3) | copy-start | bytes 1540
  12.9 462.9 %copy-start.28 = (f32[128,64]{0,1:T(8,128)}, f32[128,64]{0,1:T(8,128)S(1)}, u32[]{:S(2)}) copy-start(f32[128,64]{0,1:T(8,128)S(1)} %get-tuple-element.296) | copy-start | bytes 98308
  12.9 462.9 %copy-start.30 = (f32[128,64]{0,1:T(8,128)}, f32[128,64]{0,1:T(8,128)S(1)}, u32[]{:S(2)}) copy-start(f32[128,64]{0,1:T(8,128)S(1)} %get-tuple-element.297) | copy-start | bytes 98308
  12.9 51.4 %copy-start.60 = (f32[128]{0:T(128)S(1)}, f32[128]{0:T(128)}, u32[]{:S(2)}) copy-start(f32[128]{0:T(128)} %param.32) | copy-start | bytes 1540
  14.3 451.5 %copy-start.13 = (bf16[1,128,2048]{2,1,0:T(8,128)(2,1)}, bf16[1,128,2048]{2,1,0:T(8,128)(2,1)S(1)}, u32[]{:S(2)}) copy-start(bf16[1,128,2048]{2,1,0:T(8,128)(2,1)S(1)} %multiply_convert_fusion.7) | copy-start | bytes 1572868
  58.0 46.1 %copy-start.3 = (f32[1,128,2048]{2,1,0:T(8,128)S(1)}, f32[1,128,2048]{2,1,0:T(8,128)}, u32[]{:S(2)}) copy-start(f32[1,128,2048]{2,1,0:T(8,128)} %param.23) | copy-start | bytes 3145732
  58.0 46.1 %copy-start.45 = (f32[2048]{0:T(1024)S(1)}, f32[2048]{0:T(1024)}, u32[]{:S(2)}) copy-start(f32[2048]{0:T(1024)} %param.27) | copy-start | bytes 24580
  64.3 43.1 %copy-start.22 = (f32[128,4,128]{0,2,1:T(8,128)}, f32[128,4,128]{0,2,1:T(8,128)S(1)}, u32[]{:S(2)}) copy-start(f32[128,4,128]{0,2,1:T(8,128)S(1)} %get-tuple-element.303) | copy-start | bytes 786436
  64.4 43.1 %copy-start.54 = (f32[128,4]{0,1:T(4,128)}, f32[128,4]{0,1:T(4,128)S(1)}, u32[]{:S(2)}) copy-start(f32[128,4]{0,1:T(4,128)S(1)} %add_rsqrt_fusion.1) | copy-start | bytes 6148
  65.2 89.4 %all-gather.20.cloned.1.call-start = ((), (), s32[]{:S(2)}) async-start(), calls=%async_computation.18 | async-start | bytes 1179648 | tf_op jit(solution)/shard_map/all_gather | solution.py:129
  106.9 335.9 %all-gather.12.cloned.1.call-start = ((), (), s32[]{:S(2)}) async-start(), calls=%async_computation.14 | async-start | bytes 20971520 | tf_op jit(solution)/shard_map/all_gather | solution.py:109
  107.5 621.7 %all-gather.22.cloned.1.call-start = ((), (), s32[]{:S(2)}) async-start(), calls=%async_computation.19 | async-start | bytes 20971520 | tf_op jit(solution)/shard_map/all_gather | solution.py:112
  108.1 809.1 %all-gather.24.cloned.1.call-start = ((), (), s32[]{:S(2)}) async-start(), calls=%async_computation.20 | async-start | bytes 7864320 | tf_op jit(solution)/shard_map/all_gather | solution.py:168
  108.8 850.6 %all-gather.26.cloned.1.call-start = ((), (), s32[]{:S(2)}) async-start(), calls=%async_computation.21 | async-start | bytes 7864320 | tf_op jit(solution)/shard_map/all_gather | solution.py:169
  128.4 610.5 %copy-start.32 = (bf16[2048,16]{0,1:T(8,128)(2,1)}, bf16[2048,16]{0,1:T(8,128)(2,1)S(1)}, u32[]{:S(2)}) copy-start(bf16[2048,16]{0,1:T(8,128)(2,1)S(1)} %all_gather.48) | copy-start | bytes 196612
  133.8 332.0 %copy-start.49 = (s32[1024]{0:T(1024)}, s32[1024]{0:T(1024)S(1)}, u32[]{:S(2)}) copy-start(s32[1024]{0:T(1024)S(1)} %fusion.88) | copy-start | bytes 12292
  508.1 229.6 %copy-start.7 = (bf16[4,1024,128]{2,1,0:T(8,128)(2,1)}, bf16[4,1024,128]{2,1,0:T(8,128)(2,1)S(1)}, u32[]{:S(2)}) copy-start(bf16[4,1024,128]{2,1,0:T(8,128)(2,1)S(1)} %get-tuple-element.572) | copy-start | bytes 3145732
  508.1 229.6 %copy-start.15 = (bf16[4,8,128,128]{3,2,1,0:T(8,128)(2,1)}, bf16[4,8,128,128]{3,2,1,0:T(8,128)(2,1)S(1)}, u32[]{:S(2)}) copy-start(bf16[4,8,128,128]{3,2,1,0:T(8,128)(2,1)S(1)} %get-tuple-element.573) | copy-start | bytes 3145732
  508.1 229.6 %copy-start.34 = (s32[1024]{0:T(1024)}, s32[1024]{0:T(1024)S(1)}, u32[]{:S(2)}) copy-start(s32[1024]{0:T(1024)S(1)} %get-tuple-element.614) | copy-start | bytes 12292
  508.1 229.6 %copy-start.39 = (s32[1024]{0:T(1024)}, s32[1024]{0:T(1024)S(1)}, u32[]{:S(2)}) copy-start(s32[1024]{0:T(1024)S(1)} %get-tuple-element.630) | copy-start | bytes 12292
  508.1 229.6 %copy-start.51 = (s32[128]{0:T(128)}, s32[128]{0:T(128)S(1)}, u32[]{:S(2)}) copy-start(s32[128]{0:T(128)S(1)} %get-tuple-element.634) | copy-start | bytes 1540
  757.8 76.3 %all-to-all-start.2 = ((bf16[8,2,96,2048]{3,2,1,0:T(8,128)(2,1)}), bf16[8,2,96,2048]{3,2,1,0:T(8,128)(2,1)}, u32[]{:S(2)}, u32[]{:S(2)}) async-start(bf16[8,2,96,2048]{3,2,1,0:T(8,128)(2,1)} %bitcast.323), calls=%async_computation.2 | async-start | bytes 12582912 | tf_op jit(solution)/shard_map/all_to_all | solution.py:216
  762.6 312.0 %all-gather.28.cloned.1.call-start = ((), (), s32[]{:S(2)}) async-start(), calls=%async_computation.22 | async-start | bytes 7864320 | tf_op jit(solution)/shard_map/all_gather | solution.py:170
  834.2 76.4 %all-to-all-start = ((bf16[8,2,96,2048]{3,2,1,0:T(8,128)(2,1)}), bf16[8,2,96,2048]{3,2,1,0:T(8,128)(2,1)}, u32[]{:S(2)}, u32[]{:S(2)}) async-start(bf16[8,2,96,2048]{3,2,1,0:T(8,128)(2,1)} %bitcast.324), calls=%async_computation | async-start | bytes 12582912 | tf_op jit(solution)/shard_map/all_to_all | solution.py:191
  1114.2 76.8 %all-to-all-start.1 = ((bf16[1,2,768,2048]{3,1,0,2:T(2,128)(2,1)}), bf16[1,2,768,2048]{3,1,0,2:T(2,128)(2,1)}, u32[]{:S(2)}, u32[]{:S(2)}) async-start(bf16[1,2,768,2048]{3,1,0,2:T(2,128)(2,1)} %copy.93), calls=%async_computation.1 | async-start | bytes 12582912 | tf_op jit(solution)/shard_map/all_to_all | solution.py:204
  1190.9 76.3 %all-to-all-start.3 = ((bf16[1,2,768,2048]{3,1,0,2:T(2,128)(2,1)}), bf16[1,2,768,2048]{3,1,0,2:T(2,128)(2,1)}, u32[]{:S(2)}, u32[]{:S(2)}) async-start(bf16[1,2,768,2048]{3,1,0,2:T(2,128)(2,1)} %copy.96), calls=%async_computation.3 | async-start | bytes 12582912 | tf_op jit(solution)/shard_map/all_to_all | solution.py:231
  1195.7 213.7 %reduce-scatter.31.cloned.1.call-start = ((), (), s32[]{:S(2)}) async-start(), calls=%async_computation.32 | async-start | bytes 1179648
  1298.3 153.5 %copy-start.9 = (f32[128,2048]{1,0:T(8,128)}, f32[128,2048]{1,0:T(8,128)S(1)}, u32[]{:S(2)}) copy-start(f32[128,2048]{1,0:T(8,128)S(1)} %get-tuple-element.290) | copy-start | bytes 3145732
  1376.9 71.7 %reduce-scatter.33.cloned.1.call-start = ((), (), s32[]{:S(2)}) async-start(), calls=%async_computation.33 | async-start | bytes 1179648
  1379.2 69.3 %copy-start.4 = (f32[1,128,2048]{2,1,0:T(8,128)S(1)}, f32[1,128,2048]{2,1,0:T(8,128)}, u32[]{:S(2)}) copy-start(f32[1,128,2048]{2,1,0:T(8,128)} %param.23) | copy-start | bytes 3145732
  1379.2 69.3 %copy-start.46 = (f32[2048]{0:T(1024)S(1)}, f32[2048]{0:T(1024)}, u32[]{:S(2)}) copy-start(f32[2048]{0:T(1024)} %param.27) | copy-start | bytes 24580
  1379.2 69.3 %copy-start.59 = (f32[128]{0:T(128)S(1)}, f32[128]{0:T(128)}, u32[]{:S(2)}) copy-start(f32[128]{0:T(128)} %copy-done.58) | copy-start | bytes 1540
  1379.3 132.8 %reduce-scatter.17.cloned.1.call-start = ((), (), s32[]{:S(2)}) async-start(), calls=%async_computation.24 | async-start | bytes 2621440 | tf_op jit(solution)/shard_map/reduce_scatter | solution.py:325
  1412.9 126.6 %reduce-scatter.19.cloned.1.call-start = ((), (), s32[]{:S(2)}) async-start(), calls=%async_computation.25 | async-start | bytes 2621440 | tf_op jit(solution)/shard_map/reduce_scatter | solution.py:328
  1451.7 369.8 %reduce-scatter.21.cloned.1.call-start = ((), (), s32[]{:S(2)}) async-start(), calls=%async_computation.26 | async-start | bytes 20971520 | tf_op jit(solution)/shard_map/reduce_scatter | solution.py:331
  1461.1 643.6 %reduce-scatter.15.cloned.1.call-start = ((), (), s32[]{:S(2)}) async-start(), calls=%async_computation.23 | async-start | bytes 20971520 | tf_op jit(solution)/shard_map/reduce_scatter | solution.py:322
  1480.5 646.8 %reduce-scatter.23.cloned.1.call-start = ((), (), s32[]{:S(2)}) async-start(), calls=%async_computation.27 | async-start | bytes 81920 | tf_op jit(solution)/shard_map/reduce_scatter | solution.py:334
  1482.5 757.0 %reduce-scatter.29.cloned.1.call-start = ((), (), s32[]{:S(2)}) async-start(), calls=%async_computation.30 | async-start | bytes 7864320 | tf_op jit(solution)/shard_map/reduce_scatter | solution.py:317
  1492.2 861.3 %reduce-scatter.25.cloned.1.call-start = ((), (), s32[]{:S(2)}) async-start(), calls=%async_computation.28 | async-start | bytes 7864320 | tf_op jit(solution)/shard_map/reduce_scatter | solution.py:311
  1502.0 965.1 %reduce-scatter.27.cloned.1.call-start = ((), (), s32[]{:S(2)}) async-start(), calls=%async_computation.29 | async-start | bytes 7864320 | tf_op jit(solution)/shard_map/reduce_scatter | solution.py:314
  1511.9 1051.5 %all-reduce.4.cloned.1.call-start = ((), (), s32[]{:S(2)}) async-start(), calls=%async_computation.34 | async-start | bytes 10485760 | tf_op jit(solution)/shard_map/psum | solution.py:340
  1821.4 283.3 %copy-start.17 = (bf16[128,32,128]{0,2,1:T(8,128)(2,1)S(1)}, bf16[128,32,128]{0,2,1:T(8,128)(2,1)}, u32[]{:S(2)}) copy-start(bf16[128,32,128]{0,2,1:T(8,128)(2,1)} %multiply_convert_fusion.4) | copy-start | bytes 3145732
  1821.5 904.7 %all-gather.30.cloned.1.call-start = ((), (), s32[]{:S(2)}) async-start(), calls=%async_computation.31 | async-start | bytes 37748736 | tf_op jit(solution)/shard_map/all_gather | solution.py:339
  2116.3 38.0 %copy-start.38 = (bf16[128,512]{1,0:T(8,128)(2,1)S(1)}, bf16[128,512]{1,0:T(8,128)(2,1)}, u32[]{:S(2)}) copy-start(bf16[128,512]{1,0:T(8,128)(2,1)} %reduce-scatter.33.cloned.1.call-done) | copy-start | bytes 393220
  2151.7 46.2 %copy-start.10 = (f32[128,2048]{1,0:T(8,128)S(1)}, f32[128,2048]{1,0:T(8,128)}, u32[]{:S(2)}) copy-start(f32[128,2048]{1,0:T(8,128)} %copy-done.9) | copy-start | bytes 3145732
  (49 other events, 515.4 us)
Sparse Core Ops, SparseCore 0:
  9.6 48.3 all-gather.13
  59.6 44.4 all-gather.17
  106.5 22.2 all-gather.15
  131.1 23.3 all-gather.19
  156.0 286.7 all-gather.11
  444.2 284.9 all-gather.21
  730.7 113.5 all-gather.23
  845.8 113.5 all-gather.25
  961.0 113.5 all-gather.27
  1377.0 32.3 reduce-scatter.30
  1412.6 35.9 reduce-scatter.32
  1450.7 43.6 reduce-scatter.16
  1496.7 42.8 reduce-scatter.18
  1541.7 279.6 reduce-scatter.20
  1823.6 281.0 reduce-scatter.14
  2107.4 19.9 reduce-scatter.22
  2129.5 109.9 reduce-scatter.28
  2242.2 111.2 reduce-scatter.24
  2355.8 111.2 reduce-scatter.26
  2470.5 92.9 all-reduce.3
  2565.4 160.7 all-gather.29
